TPU v7x, 32 devices: a whole 2x2x4 slice. The times are simulated.
32 devices in a mesh: region: 2 (over y), tile: 4 (over z), corner: 2 (over x), kern: 2 (over core).
Axes of the slice: x: 2, y: 2, z: 4, core: 2. Of those that a mesh axis runs over, the one named last changes fastest.
Arguments:
- tile_mask: bfloat16 [16, 256, 256], P(('region', 'tile')), parts along dimension 0, may hold values from -1 to 1
- master_mask: bfloat16 [8, 256, 256], P(('region', 'tile')), parts along dimension 0, may hold values from -1 to 1
- target: bfloat16 [16, 256, 256], P(('region', 'tile')), parts along dimension 0, may hold values from 0 to 1
- inst_master: int32 [16], P(('region', 'tile')), parts along dimension 0, may hold values from 0 to 3, as said below
- inst_shift: int32 [16, 2], P(('region', 'tile')), parts along dimension 0, may hold values from 0 to 255
- kernels: float32 [2, 12, 2, 32, 32], P('corner'), may hold values from -24 to 24
- kernel_weight: float32 [2, 12], P('corner'), may hold values from 0.05 to 1
- corner_dose: float32 [2], P('corner'), may hold values from 0.6 to 1.6
Outputs:
- tile_grad: float32 [16, 256, 256], P(('region', 'tile')), parts along dimension 0
- master_grad: float32 [8, 256, 256], P(('region', 'tile')), parts along dimension 0
There are 2 independent parts, one for each index of `region`. A program takes and returns all parts, laid end to end along the dimension named above; an argument that names none is the same for every part. Nothing has to cross between parts.
Inputs may be any that keep to these rules, and one draw needn't show every extreme that they name: `inst_master`: each master cell is placed in exactly 2 tiles.
All inputs are finite; a program needn't handle non-finite values.
Results may differ from a plain program's by a relative error of at most 0.0003.
Values may be sent and summed in bfloat16 or wider, within the bound.
No kernel may reach another device: no remote copies, remote signals or barrier semaphores. Data moves between devices by JAX's collectives and lax.ppermute only.
A program may use at most 64 MiB of HBM per device.

v0:
```python
import math
import numpy as np
import jax
import jax.numpy as jnp
from jax import lax
from jax.sharding import PartitionSpec as P

P_SIZE = 256
B = 32
precise = lax.Precision.HIGHEST
steepness = 3.0
threshold = 1.0


def band_tables():
    freq = np.arange(B, dtype=np.int64) - B // 2
    pixel = np.arange(P_SIZE, dtype=np.int64)
    angle = (
        2.0 * math.pi / P_SIZE * np.mod(freq[:, None] * pixel[None, :], P_SIZE).astype(np.float64)
    )
    return (jnp.asarray(np.cos(angle), jnp.float32), jnp.asarray(-np.sin(angle), jnp.float32))


def phase_ramp(shift):
    freq = jnp.arange(B, dtype=jnp.int32) - B // 2
    total = (
        freq[None, :, None] * shift[:, 0][:, None, None]
        + freq[None, None, :] * shift[:, 1][:, None, None]
    )
    angle = 2.0 * math.pi / P_SIZE * jnp.mod(total, P_SIZE).astype(jnp.float32)
    return (jnp.cos(angle), -jnp.sin(angle))


def spectra(masks, cos_tab, sin_tab):
    rows_re = jnp.einsum("bx,nxy->nby", cos_tab, masks, precision=precise)
    rows_im = jnp.einsum("bx,nxy->nby", sin_tab, masks, precision=precise)
    spec_re = jnp.einsum("nby,cy->nbc", rows_re, cos_tab, precision=precise) - jnp.einsum(
        "nby,cy->nbc", rows_im, sin_tab, precision=precise
    )
    spec_im = jnp.einsum("nby,cy->nbc", rows_re, sin_tab, precision=precise) + jnp.einsum(
        "nby,cy->nbc", rows_im, cos_tab, precision=precise
    )
    return (spec_re, spec_im)


def back_pixels(x_re, x_im, cos_tab, sin_tab):
    half_re = jnp.einsum("bx,nbc->nxc", cos_tab, x_re, precision=precise) + jnp.einsum(
        "bx,nbc->nxc", sin_tab, x_im, precision=precise
    )
    half_im = jnp.einsum("bx,nbc->nxc", cos_tab, x_im, precision=precise) - jnp.einsum(
        "bx,nbc->nxc", sin_tab, x_re, precision=precise
    )
    return jnp.einsum("nxc,cy->nxy", half_re, cos_tab, precision=precise) + jnp.einsum(
        "nxc,cy->nxy", half_im, sin_tab, precision=precise
    )


def on_device(
    tile_mask, master_mask, target, inst_master, inst_shift, kernels, kernel_weight, corner_dose
):
    cos_tab, sin_tab = band_tables()
    scale = 1.0 / (P_SIZE * P_SIZE)
    local_tiles = tile_mask.shape[0]
    local_masters = master_mask.shape[0]
    tile_count = lax.axis_size("tile")
    tile_pos = lax.axis_index("tile")
    kern_count = lax.axis_size("kern")
    kern_pos = lax.axis_index("kern")
    per_dev = local_tiles // kern_count
    first = kern_pos * per_dev
    region_tiles = tile_count * local_tiles
    region_masters = tile_count * local_masters
    with jax.named_scope("master_spectra"):
        own_re, own_im = spectra(master_mask.astype(jnp.float32), cos_tab, sin_tab)
        own = jnp.stack([own_re, own_im], axis=1)
        every = lax.all_gather(own, "tile", axis=0, tiled=True)
    with jax.named_scope("tile_spectra"):
        mine_mask = lax.dynamic_slice_in_dim(tile_mask, first, per_dev, 0)
        goal = lax.dynamic_slice_in_dim(target, first, per_dev, 0).astype(jnp.float32)
        mine_master = lax.dynamic_slice_in_dim(inst_master, first, per_dev, 0)
        mine_shift = lax.dynamic_slice_in_dim(inst_shift, first, per_dev, 0)
        tile_re, tile_im = spectra(mine_mask.astype(jnp.float32), cos_tab, sin_tab)
        ph_re, ph_im = phase_ramp(mine_shift)
        pick = (
            mine_master[:, None] == jnp.arange(region_masters, dtype=jnp.int32)[None, :]
        ).astype(jnp.float32)
        sel = jnp.sum(pick[:, :, None, None, None] * every[None], axis=1)
        sel_re = sel[:, 0]
        sel_im = sel[:, 1]
        spec_re = tile_re + (ph_re * sel_re - ph_im * sel_im)
        spec_im = tile_im + (ph_re * sel_im + ph_im * sel_re)
    dose = corner_dose[0]
    h_re = kernels[0, :, 0]
    h_im = kernels[0, :, 1]
    weights = kernel_weight[0]
    with jax.named_scope("forward_fields"):
        x_re = h_re[:, None] * spec_re[None] - h_im[:, None] * spec_im[None]
        x_im = h_re[:, None] * spec_im[None] + h_im[:, None] * spec_re[None]
        half_re = jnp.einsum("bx,knbc->knxc", cos_tab, x_re, precision=precise) + jnp.einsum(
            "bx,knbc->knxc", sin_tab, x_im, precision=precise
        )
        half_im = jnp.einsum("bx,knbc->knxc", cos_tab, x_im, precision=precise) - jnp.einsum(
            "bx,knbc->knxc", sin_tab, x_re, precision=precise
        )
        f_re = (
            jnp.einsum("knxc,cy->knxy", half_re, cos_tab, precision=precise)
            + jnp.einsum("knxc,cy->knxy", half_im, sin_tab, precision=precise)
        ) * scale
        f_im = (
            jnp.einsum("knxc,cy->knxy", half_im, cos_tab, precision=precise)
            - jnp.einsum("knxc,cy->knxy", half_re, sin_tab, precision=precise)
        ) * scale
    with jax.named_scope("resist_sensitivity"):
        intensity = jnp.sum(weights[:, None, None, None] * (f_re * f_re + f_im * f_im), axis=0)
        resist = jax.nn.sigmoid(steepness * (dose * intensity - threshold))
        sens = 2.0 * (resist - goal) * resist * (1.0 - resist) * steepness * dose
    with jax.named_scope("adjoint_spectra"):
        g_re = (2.0 * weights)[:, None, None, None] * sens[None] * f_re
        g_im = (2.0 * weights)[:, None, None, None] * sens[None] * f_im
        mid_re = jnp.einsum("knxy,cy->knxc", g_re, cos_tab, precision=precise) - jnp.einsum(
            "knxy,cy->knxc", g_im, sin_tab, precision=precise
        )
        mid_im = jnp.einsum("knxy,cy->knxc", g_re, sin_tab, precision=precise) + jnp.einsum(
            "knxy,cy->knxc", g_im, cos_tab, precision=precise
        )
        out_re = (
            jnp.einsum("bx,knxc->knbc", cos_tab, mid_re, precision=precise)
            - jnp.einsum("bx,knxc->knbc", sin_tab, mid_im, precision=precise)
        ) * scale
        out_im = (
            jnp.einsum("bx,knxc->knbc", cos_tab, mid_im, precision=precise)
            + jnp.einsum("bx,knxc->knbc", sin_tab, mid_re, precision=precise)
        ) * scale
        grad_re = jnp.sum(h_re[:, None] * out_re + h_im[:, None] * out_im, axis=0)
        grad_im = jnp.sum(h_re[:, None] * out_im - h_im[:, None] * out_re, axis=0)
    with jax.named_scope("gradient_exchange"):
        back_re = ph_re * grad_re + ph_im * grad_im
        back_im = ph_re * grad_im - ph_im * grad_re
        tile_slot = tile_pos * local_tiles + first + jnp.arange(per_dev, dtype=jnp.int32)
        tile_pick = (
            tile_slot[:, None] == jnp.arange(region_tiles, dtype=jnp.int32)[None, :]
        ).astype(jnp.float32)
        own_grad = jnp.stack([grad_re, grad_im], axis=1)
        own_back = jnp.stack([back_re, back_im], axis=1)
        tile_part = jnp.sum(tile_pick[:, :, None, None, None] * own_grad[:, None], axis=0)
        master_part = jnp.sum(pick[:, :, None, None, None] * own_back[:, None], axis=0)
        slots = jnp.concatenate([tile_part, master_part], axis=0)
        summed = lax.psum(slots, ("tile", "corner", "kern"))
        mine_tiles = lax.dynamic_slice_in_dim(summed, tile_pos * local_tiles, local_tiles, 0)
        mine_masters = lax.dynamic_slice_in_dim(
            summed, region_tiles + tile_pos * local_masters, local_masters, 0
        )
    with jax.named_scope("pixel_gradients"):
        tile_grad = back_pixels(mine_tiles[:, 0], mine_tiles[:, 1], cos_tab, sin_tab)
        master_grad = back_pixels(mine_masters[:, 0], mine_masters[:, 1], cos_tab, sin_tab)
    return (tile_grad, master_grad)


def solution(mesh):
    return jax.shard_map(
        on_device,
        mesh=mesh,
        in_specs=(
            P(("region", "tile"), None, None),
            P(("region", "tile"), None, None),
            P(("region", "tile"), None, None),
            P(("region", "tile")),
            P(("region", "tile"), None),
            P("corner", None, None, None, None),
            P("corner", None),
            P("corner"),
        ),
        out_specs=(P(("region", "tile"), None, None), P(("region", "tile"), None, None)),
        check_vma=False,
    )
```

profile of v0, /device:TPU:0, one launch (start us, length us, event | category | flops | bytes accessed | tf_op | source)
XLA Modules:
  0.0 185.2 jit_solution(1260496238623281663)
XLA Ops:
  7.2 0.0 copy-start
  7.2 0.0 copy-start.6
  7.2 0.0 all-reduce.2.cloned.1.call-start
  7.3 1.1 fusion.41
  8.4 1.1 fusion.39
  9.5 0.9 fusion.81
  10.5 0.9 fusion.80
  11.4 1.0 convolution_bitcast_fusion.1
  12.4 1.0 convolution_bitcast_fusion
  13.3 0.9 fusion.79
  14.3 0.9 fusion.82
  15.2 0.7 constant_dynamic-slice_fusion
  15.9 0.6 fusion.78
  16.5 1.3 dynamic_slice.20
  17.8 0.7 compare_convert_fusion
  18.5 0.9 fusion.26
  19.4 0.9 fusion.27
  20.4 15.1 %all_gather.3 = f32[4,2,32,32]{3,2,1,0:T(8,128)S(1)} all-gather(f32[1,2,32,32]{3,2,1,0:T(8,128)S(1)} %pad_maximum_fusion.1), channel_id=1, replica_groups=mesh['region'=2,'tile'=4,'corner'=2,'kern'=2] {'tile'}, dimensions={0}, use_global_device_ids=true | all-gather | bytes 40960 | tf_op jit(solution)/shard_map/master_spectra/all_gather | solution.py:76
  35.4 1.3 fusion.75
  36.7 0.1 multiply_reduce_fusion.1
  36.8 0.9 fusion.28
  37.7 0.1 copy.17
  37.8 0.9 fusion.25
  38.8 0.1 copy.19
  38.8 1.1 fusion.77
  39.9 0.1 copy.22
  40.0 0.1 copy.23
  40.2 0.4 fusion.47
  40.6 0.5 fusion.51
  41.1 0.5 fusion.14
  41.5 0.5 fusion.15
  42.0 2.7 %fusion.83 = f32[12,256,256]{2,1,0:T(8,128)S(1)} fusion(f32[12,256,32]{1,2,0:T(8,128)S(1)} %fusion.15, f32[32,256,1]{1,0,2:T(8,128)S(1)} %copy-done.6), kind=kOutput, calls=%fused_computation.143 | convolution fusion | flops 301989888 | bytes 3571712 | tf_op jit(solution)/shard_map/forward_fields/knxc,cy->knxy/dot_general | solution.py:106
  44.8 4.3 %fusion.84 = f32[12,256,256]{2,1,0:T(8,128)} fusion(f32[12,256,32]{1,2,0:T(8,128)S(1)} %fusion.14, f32[32,256,1]{1,0,2:T(8,128)S(1)} %copy-done.6), kind=kOutput, calls=%fused_computation.144 | convolution fusion | flops 301989888 | bytes 3571712 | tf_op jit(solution)/shard_map/forward_fields/knxc,cy->knxy/dot_general | solution.py:110
  49.1 2.7 %add_multiply_fusion = f32[12,256,256]{2,1,0:T(8,128)S(1)} fusion(f32[12,256,256]{2,1,0:T(8,128)S(1)} %fusion.83, f32[12,256,32]{1,2,0:T(8,128)S(1)} %fusion.14, f32[32,256,1]{1,0,2:T(8,128)S(1)} %copy-done.5), kind=kOutput, calls=%fused_computation.4 | convolution fusion | flops 303562752 | bytes 6717440 | tf_op jit(solution)/shard_map/forward_fields/knxc,cy->knxy/dot_general | solution.py:107
  52.5 5.6 %multiply_reduce_fusion = (f32[256,256]{1,0:T(8,128)S(1)}, f32[12,256,256]{2,1,0:T(8,128)S(1)}) fusion(f32[12,256,256]{2,1,0:T(8,128)S(1)} %add_multiply_fusion, f32[12]{0:T(128)S(1)} %bitcast.235, f32[12,256,256]{2,1,0:T(8,128)} %fusion.84, f32[12,256,32]{1,2,0:T(8,128)} %copy-done.7, f32[32,256,1]{1,0,2:T(8,128)S(1)} %copy-done.5), kind=kOutput, calls=%fused_computation.2 | convolution fusion | flops 307429376 | bytes 10125360 | tf_op jit(solution)/shard_map/forward_fields/knxc,cy->knxy/dot_general | solution.py:111
  58.1 0.1 fusion.32
  58.3 3.3 %fusion = f32[12,256,32]{1,2,0:T(8,128)S(1)} fusion(f32[32,256,1]{1,0,2:T(8,128)S(1)} %copy-done.5, f32[12,256,256]{2,1,0:T(8,128)S(1)} %add_multiply_fusion, f32[256,256]{1,0:T(8,128)S(1)} %fusion.32, f32[12]{0:T(128)S(1)} %broadcast_multiply_fusion.2), kind=kOutput, calls=%fused_computation.5 | convolution fusion | flops 303562752 | bytes 3833904 | tf_op jit(solution)/shard_map/adjoint_spectra/knxy,cy->knxc/dot_general | solution.py:123
  61.6 3.3 %fusion.1 = f32[12,256,32]{1,2,0:T(8,128)S(1)} fusion(f32[32,256,1]{1,0,2:T(8,128)S(1)} %copy-done.6, f32[12,256,256]{2,1,0:T(8,128)S(1)} %add_multiply_fusion, f32[256,256]{1,0:T(8,128)S(1)} %fusion.32, f32[12]{0:T(128)S(1)} %broadcast_multiply_fusion.2), kind=kOutput, calls=%fused_computation.6 | convolution fusion | flops 303562752 | bytes 3833904 | tf_op jit(solution)/shard_map/adjoint_spectra/knxy,cy->knxc/dot_general | solution.py:120
  64.8 3.3 %fusion.13 = f32[12,256,32]{1,2,0:T(8,128)S(1)} fusion(f32[12,256,32]{1,2,0:T(8,128)S(1)} %fusion, f32[32,256,1]{1,0,2:T(8,128)S(1)} %copy-done.6, f32[12,256,256]{2,1,0:T(8,128)S(1)} %get-tuple-element.11, f32[256,256]{1,0:T(8,128)S(1)} %fusion.32, f32[12]{0:T(128)S(1)} %broadcast_multiply_fusion.2), kind=kOutput, calls=%fused_computation.19 | convolution fusion | flops 303661056 | bytes 4227120 | tf_op jit(solution)/shard_map/adjoint_spectra/knxy,cy->knxc/dot_general | solution.py:123
  68.2 3.5 %fusion.12 = f32[12,256,32]{1,2,0:T(8,128)S(1)} fusion(f32[12,256,32]{1,2,0:T(8,128)S(1)} %fusion.1, f32[32,256,1]{1,0,2:T(8,128)S(1)} %copy-done.5, f32[12,256,256]{2,1,0:T(8,128)S(1)} %get-tuple-element.11, f32[256,256]{1,0:T(8,128)S(1)} %fusion.32, f32[12]{0:T(128)S(1)} %broadcast_multiply_fusion.2), kind=kOutput, calls=%fused_computation.18 | convolution fusion | flops 303661056 | bytes 4227120 | tf_op jit(solution)/shard_map/adjoint_spectra/knxy,cy->knxc/dot_general | solution.py:120
  71.7 0.5 fusion.85
  72.1 0.5 fusion.86
  72.6 0.5 fusion.20
  73.1 0.5 fusion.34
  73.6 0.2 multiply_add_fusion
  73.7 0.1 copy.20
  73.8 0.1 copy.21
  73.9 0.1 broadcast_multiply_fusion.1
  74.0 0.1 broadcast_multiply_fusion
  74.1 0.8 pad_maximum_fusion
  74.9 0.0 all-reduce.2.cloned.1.call-update
  74.9 91.9 %all-reduce.2.cloned.1.call-done = f32[12,2,32,32]{3,2,1,0:T(8,128)} async-done(((f32[12,2,32,32]{3,2,1,0:T(8,128)}), f32[12,2,32,32]{3,2,1,0:T(8,128)}) %all-reduce.2.cloned.1.call-update) | async-done | bytes 98320 | tf_op jit(solution)/shard_map/gradient_exchange/psum | solution.py:148
  166.8 0.9 fusion.61
  167.8 0.9 fusion.24
  168.7 0.4 fusion.88
  169.2 1.0 fusion.53
  170.2 1.0 fusion.22
  171.2 0.6 fusion.87
  171.8 0.9 fusion.62
  172.8 0.9 fusion.23
  173.7 1.1 fusion.16
  174.9 1.0 fusion.54
  175.9 1.0 fusion.21
  176.9 1.4 convolution_add_fusion
  (27 shorter events, 0.1 us)
Async XLA Ops:
  7.2 4.2 %copy-start = (bf16[2,256,256]{2,1,0:T(8,128)(2,1)S(1)}, bf16[2,256,256]{2,1,0:T(8,128)(2,1)}, u32[]{:S(2)}) copy-start(bf16[2,256,256]{2,1,0:T(8,128)(2,1)} %param.10) | copy-start | bytes 786436
  7.2 33.0 %copy-start.6 = (f32[32,256,1]{1,0,2:T(8,128)S(1)}, f32[32,256,1]{1,0,2:T(8,128)}, u32[]{:S(2)}) copy-start(f32[32,256,1]{1,0,2:T(8,128)} %constant.68) | copy-start | bytes 98308
  7.2 33.9 %copy-start.5 = (f32[32,256,1]{1,0,2:T(8,128)S(1)}, f32[32,256,1]{1,0,2:T(8,128)}, u32[]{:S(2)}) copy-start(f32[32,256,1]{1,0,2:T(8,128)} %constant.69) | copy-start | bytes 98308
  7.2 159.6 %all-reduce.2.cloned.1.call-start = ((), (), s32[]{:S(2)}) async-start(), calls=%async_computation | async-start | bytes 786432 | tf_op jit(solution)/shard_map/gradient_exchange/psum | solution.py:148
  40.0 4.8 %copy-start.1 = (f32[1,12,1,32,32]{3,4,1,2,0:T(8,128)}, f32[1,12,1,32,32]{3,4,1,2,0:T(8,128)S(1)}, u32[]{:S(2)}) copy-start(f32[1,12,1,32,32]{3,4,1,2,0:T(8,128)S(1)} %copy.22) | copy-start | bytes 147460
  40.1 4.6 %copy-start.3 = (f32[1,12,1,32,32]{3,4,1,2,0:T(8,128)}, f32[1,12,1,32,32]{3,4,1,2,0:T(8,128)S(1)}, u32[]{:S(2)}) copy-start(f32[1,12,1,32,32]{3,4,1,2,0:T(8,128)S(1)} %copy.23) | copy-start | bytes 147460
  42.0 2.8 %copy-start.7 = (f32[12,256,32]{1,2,0:T(8,128)}, f32[12,256,32]{1,2,0:T(8,128)S(1)}, u32[]{:S(2)}) copy-start(f32[12,256,32]{1,2,0:T(8,128)S(1)} %fusion.15) | copy-start | bytes 1179652
  49.1 3.4 %copy-start.11 = (f32[1,12]{1,0:T(1,128)S(1)}, f32[1,12]{1,0:T(1,128)}, u32[]{:S(2)}) copy-start(f32[1,12]{1,0:T(1,128)} %param.16) | copy-start | bytes 148
  52.5 5.6 %copy-start.10 = (bf16[2,256,256]{2,1,0:T(8,128)(2,1)S(1)}, bf16[2,256,256]{2,1,0:T(8,128)(2,1)}, u32[]{:S(2)}) copy-start(bf16[2,256,256]{2,1,0:T(8,128)(2,1)} %param.12) | copy-start | bytes 786436
  68.1 4.9 %copy-start.2 = (f32[1,12,1,32,32]{3,4,1,2,0:T(8,128)S(1)}, f32[1,12,1,32,32]{3,4,1,2,0:T(8,128)}, u32[]{:S(2)}) copy-start(f32[1,12,1,32,32]{3,4,1,2,0:T(8,128)} %copy-done.1) | copy-start | bytes 147460
  68.1 4.9 %copy-start.4 = (f32[1,12,1,32,32]{3,4,1,2,0:T(8,128)S(1)}, f32[1,12,1,32,32]{3,4,1,2,0:T(8,128)}, u32[]{:S(2)}) copy-start(f32[1,12,1,32,32]{3,4,1,2,0:T(8,128)} %copy-done.3) | copy-start | bytes 147460
  71.6 95.2 %copy-start.9 = (f32[32,256]{1,0:T(8,128)S(1)}, f32[32,256]{1,0:T(8,128)}, u32[]{:S(2)}) copy-start(f32[32,256]{1,0:T(8,128)} %constant.58.clone) | copy-start | bytes 98308
  71.7 96.1 %copy-start.8 = (f32[32,256]{1,0:T(8,128)S(1)}, f32[32,256]{1,0:T(8,128)}, u32[]{:S(2)}) copy-start(f32[32,256]{1,0:T(8,128)} %constant.59.clone) | copy-start | bytes 98308
Sparse Core Ops, SparseCore 0:
  75.0 91.7 all-reduce.1
where the time goes:
time: 187 us; the launch traced here: 185 us
  waiting for transfers between devices  91.9 us (49%)
  matrix products  55.3 us (30%)
  between operations  15.2 us (8%)
  blocking collectives  15.1 us (8%)
  local copies, waits for them, and re-layouts  4.24 us (2%)
  other arithmetic  3.34 us (2%)
    psum x1, waiting for transfers between devices, on_device(): summed = lax.psum(slots, ('tile', 'corner', 'kern'))  91.9 us
    all_gather x1, blocking collectives, on_device(): every = lax.all_gather(own, 'tile', axis=0, tiled=True)  15.1 us
    dot_general x1, matrix products, on_device(): jnp.einsum('knxc,cy->knxy', half_re, sin_tab, precision=precise)  5.58 us
    dot_general x1, matrix products, on_device(): jnp.einsum('knxc,cy->knxy', half_im, cos_tab, precision=precise)  4.34 us
  transfers between devices with their start and end apart: 1, of which 1 were waited for; matrix products, arithmetic and copies ran while one was open for 0% of the time, Pallas kernels for 0%

commit v1 on v0

--- a/solution.py
+++ b/solution.py
@@ -4,6 +4,7 @@
 import jax.numpy as jnp
 from jax import lax
 from jax.sharding import PartitionSpec as P
+from jax.lax import axis_index, axis_size, ppermute
 
 P_SIZE = 256
 B = 32
@@ -73,7 +74,35 @@
     with jax.named_scope("master_spectra"):
         own_re, own_im = spectra(master_mask.astype(jnp.float32), cos_tab, sin_tab)
         own = jnp.stack([own_re, own_im], axis=1)
-        every = lax.all_gather(own, "tile", axis=0, tiled=True)
+
+        def stops_all_carry(vals):
+            local_out = axis_index("tile")
+            placed = axis_size("tile")
+            carry, z_new, met_up = (placed, local_out, vals.shape[0])
+            item_now = jnp.zeros(
+                [k0 * carry if dev == 0 else k0 for dev, k0 in enumerate(vals.shape)], vals.dtype
+            )
+            arr_out = lax.dynamic_update_slice_in_dim(item_now, vals, z_new * met_up, axis=0)
+            z = near = vals
+            for src_i in range(1, carry // 2 + 1):
+                z = ppermute(
+                    z, axis_name="tile", perm=[(dev, (dev + 1) % carry) for dev in range(carry)]
+                )
+                arr_out = lax.dynamic_update_slice_in_dim(
+                    arr_out, z, (z_new - src_i) % carry * met_up, axis=0
+                )
+                if 2 * src_i < carry:
+                    near = ppermute(
+                        near,
+                        axis_name="tile",
+                        perm=[(dev, (dev - 1) % carry) for dev in range(carry)],
+                    )
+                    arr_out = lax.dynamic_update_slice_in_dim(
+                        arr_out, near, (z_new + src_i) % carry * met_up, axis=0
+                    )
+            return arr_out
+
+        every = stops_all_carry(own)
     with jax.named_scope("tile_spectra"):
         mine_mask = lax.dynamic_slice_in_dim(tile_mask, first, per_dev, 0)
         goal = lax.dynamic_slice_in_dim(target, first, per_dev, 0).astype(jnp.float32)

time: 187 us -> 175 us (0.936)
  blocking collectives: 15.1 us -> 0 us
  starting transfers between devices: 0.04 us -> 5.26 us
  matrix products: 55.3 us -> 50.3 us
  waiting for transfers between devices: 91.9 us -> 94.6 us
    all_gather x1 -> x0, blocking collectives: 15.1 us -> none  [on_device(): every = lax.all_gather(own, 'tile', axis=0, tiled=True)]
    ppermute x0 -> x3, waiting for transfers between devices: none -> 5.66 us  [the longest x2 5.66 us: stops_all_carry(): ppermute(z, axis_name='tile', perm=[(dev, (dev + 1) % carry) for dev in r...]
    ppermute x0 -> x3, starting transfers between devices: none -> 5.22 us  [the longest x2 3.14 us: stops_all_carry(): ppermute(z, axis_name='tile', perm=[(dev, (dev + 1) % carry) for dev in r...]
    psum x1, waiting for transfers between devices: 91.9 us -> 88.9 us  [on_device(): summed = lax.psum(slots, ('tile', 'corner', 'kern'))]
    dot_general x1, matrix products: 5.58 us -> 3.6 us  [on_device(): jnp.einsum('knxc,cy->knxy', half_re, sin_tab, precision=precise)]
  transfers between devices with their start and end apart: 1 -> 4, of which waited for: 1 -> 2; matrix products, arithmetic and copies ran while one was open for 0% -> 6% of each run, Pallas kernels for 0% -> 0%
where the time goes in v1:
time: 175 us; the launch traced here: 174 us
  waiting for transfers between devices  94.6 us (54%)
  matrix products  50.3 us (29%)
  between operations  15.3 us (9%)
  starting transfers between devices  5.26 us (3%)
  local copies, waits for them, and re-layouts  4.16 us (2%)
  other arithmetic  3.97 us (2%)
    psum x1, waiting for transfers between devices, on_device(): summed = lax.psum(slots, ('tile', 'corner', 'kern'))  88.9 us
    ppermute x2, waiting for transfers between devices, stops_all_carry(): ppermute(z, axis_name='tile', perm=[(dev, (dev + 1) % carry) for dev in r...  5.66 us
    dot_general x1, matrix products, on_device(): jnp.einsum('knxc,cy->knxy', half_re, sin_tab, precision=precise)  3.6 us
  transfers between devices with their start and end apart: 4, of which 2 were waited for; matrix products, arithmetic and copies ran while one was open for 6% of the time, Pallas kernels for 0%

profile of v1, /device:TPU:0, one launch (start us, length us, event | category | flops | bytes accessed | tf_op | source)
XLA Modules:
  0.0 173.6 jit_solution(4019067566712141208)
XLA Ops:
  7.3 1.2 fusion.41
  8.4 1.1 fusion.39
  9.6 0.9 fusion.81
  10.5 0.9 fusion.80
  11.4 0.9 fusion.26
  12.3 0.9 fusion.27
  13.3 3.1 %collective-permute-start = (f32[1,2,32,32]{3,2,1,0:T(8,128)S(1)}, f32[1,2,32,32]{3,2,1,0:T(8,128)S(1)}, u32[]{:S(2)}, u32[]{:S(2)}) collective-permute-start(f32[1,2,32,32]{3,2,1,0:T(8,128)S(1)} %pad_maximum_fusion.1), channel_id=1, source_target_pairs={{0,4},{4,8},{8,12},{12,0},{1,5},{5,9},{9,13},{13,1},{2,6},{6,10},{... | collective-permute-start | bytes 24584 | tf_op jit(solution)/shard_map/master_spectra/ppermute | solution.py:88
  16.4 2.1 %collective-permute-start.1 = (f32[1,2,32,32]{3,2,1,0:T(8,128)S(1)}, f32[1,2,32,32]{3,2,1,0:T(8,128)S(1)}, u32[]{:S(2)}, u32[]{:S(2)}) collective-permute-start(f32[1,2,32,32]{3,2,1,0:T(8,128)S(1)} %pad_maximum_fusion.1), channel_id=1, source_target_pairs={{0,12},{4,0},{8,4},{12,8},{1,13},{5,1},{9,5},{13,9},{2,14},{6,2},{... | collective-permute-start | bytes 24584 | tf_op jit(solution)/shard_map/master_spectra/ppermute | solution.py:95
  18.5 1.0 convolution_bitcast_fusion.1
  19.4 1.0 convolution_bitcast_fusion
  20.4 0.9 fusion.79
  21.3 0.9 fusion.82
  22.2 1.2 dynamic_slice.20
  23.5 0.6 compare_convert_fusion
  24.1 0.7 constant_dynamic-slice_fusion
  24.8 0.6 fusion.78
  25.4 1.0 fusion.77
  26.5 0.7 broadcast_multiply_fusion.2
  27.2 1.3 fusion.75
  28.5 0.1 copy.22
  28.7 0.1 copy.23
  29.5 0.1 collective-permute-start.2
  29.6 5.7 %collective-permute-done.2 = f32[1,2,32,32]{3,2,1,0:T(8,128)S(1)} collective-permute-done((f32[1,2,32,32]{3,2,1,0:T(8,128)S(1)}, f32[1,2,32,32]{3,2,1,0:T(8,128)S(1)}, u32[]{:S(2)}, u32[]{:S(2)}) %collective-permute-start.2) | collective-permute-done | bytes 8224 | tf_op jit(solution)/shard_map/master_spectra/ppermute | solution.py:88
  35.2 0.1 multiply_reduce_fusion.1
  35.3 0.2 fusion.28
  35.5 0.1 copy.17
  35.6 0.2 fusion.25
  35.8 0.1 copy.19
  35.8 0.5 fusion.47
  36.3 0.5 fusion.51
  36.8 0.5 fusion.14
  37.2 0.5 fusion.15
  37.7 2.8 %fusion.83 = f32[12,256,256]{2,1,0:T(8,128)S(1)} fusion(f32[12,256,32]{1,2,0:T(8,128)S(1)} %fusion.15, f32[32,256,1]{1,0,2:T(8,128)S(1)} %copy-done.2), kind=kOutput, calls=%fused_computation.147 | convolution fusion | flops 301989888 | bytes 3571712 | tf_op jit(solution)/shard_map/forward_fields/knxc,cy->knxy/dot_general | solution.py:135
  40.5 2.8 %fusion.84 = f32[12,256,256]{2,1,0:T(8,128)S(1)} fusion(f32[12,256,32]{1,2,0:T(8,128)S(1)} %fusion.14, f32[32,256,1]{1,0,2:T(8,128)S(1)} %copy-done.2), kind=kOutput, calls=%fused_computation.148 | convolution fusion | flops 301989888 | bytes 3571712 | tf_op jit(solution)/shard_map/forward_fields/knxc,cy->knxy/dot_general | solution.py:139
  43.3 2.8 %add_multiply_fusion = f32[12,256,256]{2,1,0:T(8,128)S(1)} fusion(f32[12,256,256]{2,1,0:T(8,128)S(1)} %fusion.83, f32[12,256,32]{1,2,0:T(8,128)S(1)} %fusion.14, f32[32,256,1]{1,0,2:T(8,128)S(1)} %copy-done.1), kind=kOutput, calls=%fused_computation.4 | convolution fusion | flops 303562752 | bytes 6717440 | tf_op jit(solution)/shard_map/forward_fields/knxc,cy->knxy/dot_general | solution.py:136
  46.1 3.6 %multiply_reduce_fusion = (f32[256,256]{1,0:T(8,128)S(1)}, f32[12,256,256]{2,1,0:T(8,128)S(1)}) fusion(f32[12,256,256]{2,1,0:T(8,128)S(1)} %add_multiply_fusion, f32[12]{0:T(128)S(1)} %bitcast.243, f32[12,256,256]{2,1,0:T(8,128)S(1)} %fusion.84, f32[12,256,32]{1,2,0:T(8,128)S(1)} %fusion.15, f32[32,256,1]{1,0,2:T(8,128)S(1)} %copy-done.1), kind=kOutput, calls=%fused_computation.2 | convolution fusion | flops 307429376 | bytes 10125360 | tf_op jit(solution)/shard_map/forward_fields/knxc,cy->knxy/dot_general | solution.py:140
  49.7 0.1 fusion.32
  49.8 3.3 %fusion = f32[12,256,32]{1,2,0:T(8,128)S(1)} fusion(f32[32,256,1]{1,0,2:T(8,128)S(1)} %copy-done.1, f32[12,256,256]{2,1,0:T(8,128)S(1)} %add_multiply_fusion, f32[256,256]{1,0:T(8,128)S(1)} %fusion.32, f32[12]{0:T(128)S(1)} %broadcast_multiply_fusion.2), kind=kOutput, calls=%fused_computation.5 | convolution fusion | flops 303562752 | bytes 3833904 | tf_op jit(solution)/shard_map/adjoint_spectra/knxy,cy->knxc/dot_general | solution.py:152
  53.1 3.3 %fusion.1 = f32[12,256,32]{1,2,0:T(8,128)S(1)} fusion(f32[32,256,1]{1,0,2:T(8,128)S(1)} %copy-done.2, f32[12,256,256]{2,1,0:T(8,128)S(1)} %add_multiply_fusion, f32[256,256]{1,0:T(8,128)S(1)} %fusion.32, f32[12]{0:T(128)S(1)} %broadcast_multiply_fusion.2), kind=kOutput, calls=%fused_computation.6 | convolution fusion | flops 303562752 | bytes 3833904 | tf_op jit(solution)/shard_map/adjoint_spectra/knxy,cy->knxc/dot_general | solution.py:149
  56.4 3.3 %fusion.13 = f32[12,256,32]{1,2,0:T(8,128)S(1)} fusion(f32[12,256,32]{1,2,0:T(8,128)S(1)} %fusion, f32[32,256,1]{1,0,2:T(8,128)S(1)} %copy-done.2, f32[12,256,256]{2,1,0:T(8,128)S(1)} %get-tuple-element.11, f32[256,256]{1,0:T(8,128)S(1)} %fusion.32, f32[12]{0:T(128)S(1)} %broadcast_multiply_fusion.2), kind=kOutput, calls=%fused_computation.19 | convolution fusion | flops 303661056 | bytes 4227120 | tf_op jit(solution)/shard_map/adjoint_spectra/knxy,cy->knxc/dot_general | solution.py:152
  59.7 3.3 %fusion.12 = f32[12,256,32]{1,2,0:T(8,128)S(1)} fusion(f32[12,256,32]{1,2,0:T(8,128)S(1)} %fusion.1, f32[32,256,1]{1,0,2:T(8,128)S(1)} %copy-done.1, f32[12,256,256]{2,1,0:T(8,128)S(1)} %get-tuple-element.11, f32[256,256]{1,0:T(8,128)S(1)} %fusion.32, f32[12]{0:T(128)S(1)} %broadcast_multiply_fusion.2), kind=kOutput, calls=%fused_computation.18 | convolution fusion | flops 303661056 | bytes 4227120 | tf_op jit(solution)/shard_map/adjoint_spectra/knxy,cy->knxc/dot_general | solution.py:149
  63.0 0.7 fusion.85
  63.6 0.5 fusion.86
  64.1 0.5 fusion.20
  64.6 0.5 fusion.34
  65.0 0.2 multiply_add_fusion
  65.2 0.1 copy.20
  65.3 0.1 copy.21
  65.4 0.1 broadcast_multiply_fusion.1
  65.5 0.1 broadcast_multiply_fusion
  65.5 0.8 pad_maximum_fusion
  66.4 88.9 %all-reduce.2.cloned.1.call-done = f32[12,2,32,32]{3,2,1,0:T(8,128)} async-done(((f32[12,2,32,32]{3,2,1,0:T(8,128)}), f32[12,2,32,32]{3,2,1,0:T(8,128)}) %all-reduce.2.cloned.1.call-update) | async-done | bytes 98320 | tf_op jit(solution)/shard_map/gradient_exchange/psum | solution.py:177
  155.3 0.9 fusion.61
  156.2 0.9 fusion.24
  157.2 0.4 fusion.88
  157.6 1.0 fusion.53
  158.6 1.0 fusion.22
  159.7 0.6 fusion.87
  160.3 0.9 fusion.62
  161.2 0.9 fusion.23
  162.2 1.1 fusion.16
  163.3 1.0 fusion.54
  164.3 1.0 fusion.21
  165.4 1.4 convolution_add_fusion
  (27 shorter events, 0.2 us)
Async XLA Ops:
  7.2 11.3 %copy-start = (bf16[2,256,256]{2,1,0:T(8,128)(2,1)S(1)}, bf16[2,256,256]{2,1,0:T(8,128)(2,1)}, u32[]{:S(2)}) copy-start(bf16[2,256,256]{2,1,0:T(8,128)(2,1)} %param.10) | copy-start | bytes 786436
  7.2 28.4 %copy-start.4 = (f32[32,256]{1,0:T(8,128)S(1)}, f32[32,256]{1,0:T(8,128)}, u32[]{:S(2)}) copy-start(f32[32,256]{1,0:T(8,128)} %constant.89.clone) | copy-start | bytes 98308
  7.2 28.1 %copy-start.3 = (f32[32,256]{1,0:T(8,128)S(1)}, f32[32,256]{1,0:T(8,128)}, u32[]{:S(2)}) copy-start(f32[32,256]{1,0:T(8,128)} %constant.90.clone) | copy-start | bytes 98308
  7.2 28.6 %copy-start.2 = (f32[32,256,1]{1,0,2:T(8,128)S(1)}, f32[32,256,1]{1,0,2:T(8,128)}, u32[]{:S(2)}) copy-start(f32[32,256,1]{1,0,2:T(8,128)} %constant.99) | copy-start | bytes 98308
  7.2 29.5 %copy-start.1 = (f32[32,256,1]{1,0,2:T(8,128)S(1)}, f32[32,256,1]{1,0,2:T(8,128)}, u32[]{:S(2)}) copy-start(f32[32,256,1]{1,0,2:T(8,128)} %constant.100) | copy-start | bytes 98308
  7.2 148.1 %all-reduce.2.cloned.1.call-start = ((), (), s32[]{:S(2)}) async-start(), calls=%async_computation | async-start | bytes 786432 | tf_op jit(solution)/shard_map/gradient_exchange/psum | solution.py:177
  13.3 16.2 %collective-permute-start = (f32[1,2,32,32]{3,2,1,0:T(8,128)S(1)}, f32[1,2,32,32]{3,2,1,0:T(8,128)S(1)}, u32[]{:S(2)}, u32[]{:S(2)}) collective-permute-start(f32[1,2,32,32]{3,2,1,0:T(8,128)S(1)} %pad_maximum_fusion.1), channel_id=1, source_target_pairs={{0,4},{4,8},{8,12},{12,0},{1,5},{5,9},{9,13},{13,1},{2,6},{6,10},{... | collective-permute-start | bytes 24584 | tf_op jit(solution)/shard_map/master_spectra/ppermute | solution.py:88
  16.4 13.2 %collective-permute-start.1 = (f32[1,2,32,32]{3,2,1,0:T(8,128)S(1)}, f32[1,2,32,32]{3,2,1,0:T(8,128)S(1)}, u32[]{:S(2)}, u32[]{:S(2)}) collective-permute-start(f32[1,2,32,32]{3,2,1,0:T(8,128)S(1)} %pad_maximum_fusion.1), channel_id=1, source_target_pairs={{0,12},{4,0},{8,4},{12,8},{1,13},{5,1},{9,5},{13,9},{2,14},{6,2},{... | collective-permute-start | bytes 24584 | tf_op jit(solution)/shard_map/master_spectra/ppermute | solution.py:95
  29.5 5.8 %collective-permute-start.2 = (f32[1,2,32,32]{3,2,1,0:T(8,128)S(1)}, f32[1,2,32,32]{3,2,1,0:T(8,128)S(1)}, u32[]{:S(2)}, u32[]{:S(2)}) collective-permute-start(f32[1,2,32,32]{3,2,1,0:T(8,128)S(1)} %collective-permute-done), channel_id=1, source_target_pairs={{0,4},{4,8},{8,12},{12,0},{1,5},{5,9},{9,13},{13,1},{2,6},{6,10},{... | collective-permute-start | bytes 24584 | tf_op jit(solution)/shard_map/master_spectra/ppermute | solution.py:88
  43.3 2.8 %copy-start.6 = (f32[1,12]{1,0:T(1,128)S(1)}, f32[1,12]{1,0:T(1,128)}, u32[]{:S(2)}) copy-start(f32[1,12]{1,0:T(1,128)} %param.16) | copy-start | bytes 148
  46.0 3.6 %copy-start.5 = (bf16[2,256,256]{2,1,0:T(8,128)(2,1)S(1)}, bf16[2,256,256]{2,1,0:T(8,128)(2,1)}, u32[]{:S(2)}) copy-start(bf16[2,256,256]{2,1,0:T(8,128)(2,1)} %param.12) | copy-start | bytes 786436
Sparse Core Ops, SparseCore 0:
  66.5 88.7 all-reduce.1
